TPU v7x, 256 devices: a whole 4x4x8 slice. The times are simulated.
256 devices in a mesh: dp: 32 (over z_lo, y, core), graph: 8 (over z_hi, x).
Axes of the slice: x: 4, y: 4, z: 8 (z_hi: 2, z_lo: 4; z = z_hi * 4 + z_lo), core: 2. Of those that a mesh axis runs over, the one named last changes fastest.
Arguments:
- embedding: bfloat16 [32, 12288, 512], P('dp', 'graph'), may hold values from -6 to 6
- triplet_basis: bfloat16 [32, 49152, 64], P('dp', 'graph'), may hold values from -6 to 6
- atom_cotangent: bfloat16 [32, 768, 1024], P('dp', 'graph'), may hold values from -6 to 6
- fidelity: int32 [32, 768], P('dp', 'graph'), may hold values 0 or 1
- edge_target: int32 [32, 12288], P('dp', 'graph'), may hold values from 0 to 767, as said below
- triplet_source: int32 [32, 49152], P('dp', 'graph'), may hold values from 0 to 12287, as said below
- triplet_target: int32 [32, 49152], P('dp', 'graph'), may hold values from 0 to 12287, as said below
- edge_count: int32 [32, 8], P('dp', 'graph'), may hold values from 768 to 1536, as said below
- triplet_count: int32 [32, 8], P('dp', 'graph'), may hold values from 1536 to 6144, as said below
- w_down: bfloat16 [512, 64], replicated, may hold values from -0.25 to 0.25
- w_up: bfloat16 [64, 512], replicated, may hold values from -0.75 to 0.75
- w_atom: bfloat16 [512, 1024], replicated, may hold values from -0.25 to 0.25
Outputs:
- embedding_grad: bfloat16 [32, 12288, 512], P('dp', 'graph')
- w_atom_grad: float32 [512, 1024], P(None, 'graph')
- w_up_grad: float32 [64, 512], replicated
- w_down_grad: float32 [512, 64], replicated
Inputs may be any that keep to these rules, and one draw needn't show every extreme that they name: `edge_target`: edges of index g of graph, slots g * 1536 to (g + 1) * 1536 - 1, have target atoms anywhere in their batch. `triplet_source`: A live edge slot of any index of graph in the same batch. `triplet_target`: A live edge slot of the same index of graph as the triplet slot. `edge_count`: some index of graph of every batch has all 1536 edge slots live. `triplet_count`: some index of graph of every batch has all 6144 triplet slots live.
All inputs are finite; a program needn't handle non-finite values. No bound on the sum of `fidelity` on one device may be relied on, other than what follows from the above.
Results may differ from a plain program's by a relative error of at most 0.0077.
Values may be sent and summed in bfloat16 or wider, within the bound.
No kernel may reach another device: no remote copies, remote signals or barrier semaphores. Data moves between devices by JAX's collectives and lax.ppermute only.
A program may use at most 128 MiB of HBM per device.

v0:
```python
import jax
import jax.numpy as jnp
from jax import lax
from jax.sharding import PartitionSpec as P


def local(
    embedding,
    triplet_basis,
    atom_cotangent,
    fidelity,
    edge_target,
    triplet_source,
    triplet_target,
    edge_count,
    triplet_count,
    w_down,
    w_up,
    w_atom,
):
    rows = embedding[0]
    basis = triplet_basis[0]
    edge_slots = rows.shape[0]
    trip_slots = basis.shape[0]
    groups = lax.axis_size("graph")
    here = lax.axis_index("graph")
    edge_live = jnp.arange(edge_slots, dtype=jnp.int32) < edge_count[0, 0]
    trip_live = jnp.arange(trip_slots, dtype=jnp.int32) < triplet_count[0, 0]
    weight = 1.0 + 3.0 * fidelity[0].astype(jnp.float32)
    scaled = (weight[:, None] * atom_cotangent[0].astype(jnp.float32)).astype(jnp.bfloat16)
    atoms_all = lax.all_gather(scaled, "graph", axis=0, tiled=True)
    projected = jnp.dot(rows, w_down, preferred_element_type=jnp.float32).astype(jnp.bfloat16)
    table = lax.all_gather(projected, "graph", axis=0, tiled=True)
    feats = jnp.take(table, triplet_source[0], axis=0)
    local_dest = triplet_target[0] - here * edge_slots
    product = jnp.where(
        trip_live[:, None], feats.astype(jnp.float32) * basis.astype(jnp.float32), jnp.float32(0.0)
    )
    aggregate = jax.ops.segment_sum(product, local_dest, num_segments=edge_slots).astype(
        jnp.bfloat16
    )
    pre = jnp.dot(aggregate, w_up, preferred_element_type=jnp.float32)
    sig = jax.nn.sigmoid(pre)
    updated = (rows.astype(jnp.float32) + pre * sig).astype(jnp.bfloat16)
    edge_in = jnp.where(
        edge_live[:, None], jnp.take(atoms_all, edge_target[0], axis=0), jnp.zeros((), jnp.bfloat16)
    )
    edge_out = jnp.dot(edge_in, w_atom.T, preferred_element_type=jnp.float32)
    part_atom = jnp.dot(updated.T, edge_in, preferred_element_type=jnp.float32)
    pre_grad = (edge_out * sig * (1.0 + pre * (1.0 - sig))).astype(jnp.bfloat16)
    part_up = jnp.dot(aggregate.T, pre_grad, preferred_element_type=jnp.float32)
    aggregate_grad = jnp.dot(pre_grad, w_up.T, preferred_element_type=jnp.float32).astype(
        jnp.bfloat16
    )
    contrib = jnp.where(
        trip_live[:, None],
        jnp.take(aggregate_grad, local_dest, axis=0).astype(jnp.float32)
        * basis.astype(jnp.float32),
        jnp.float32(0.0),
    )
    partial_grad = jax.ops.segment_sum(
        contrib, triplet_source[0], num_segments=edge_slots * groups
    ).astype(jnp.bfloat16)
    source_grad = (
        lax.psum_scatter(partial_grad, "graph", scatter_dimension=0, tiled=True)
        .astype(jnp.float32)
        .astype(jnp.bfloat16)
    )
    part_down = jnp.dot(rows.T, source_grad, preferred_element_type=jnp.float32)
    result = (edge_out + jnp.dot(source_grad, w_down.T, preferred_element_type=jnp.float32)).astype(
        jnp.bfloat16
    )
    total_atom, up_grad, down_grad = lax.psum((part_atom, part_up, part_down), ("dp", "graph"))
    width = total_atom.shape[1] // groups
    atom_grad = lax.dynamic_slice_in_dim(total_atom, here * width, width, 1)
    return (result[None], atom_grad, up_grad, down_grad)


def solution(mesh):
    return jax.shard_map(
        local,
        mesh=mesh,
        in_specs=(
            P("dp", "graph", None),
            P("dp", "graph", None),
            P("dp", "graph", None),
            P("dp", "graph"),
            P("dp", "graph"),
            P("dp", "graph"),
            P("dp", "graph"),
            P("dp", "graph"),
            P("dp", "graph"),
            P(),
            P(),
            P(),
        ),
        out_specs=(P("dp", "graph", None), P(None, "graph"), P(), P()),
        check_vma=False,
    )
```

profile of v0, /device:TPU:8, one launch (start us, length us, event | category | flops | bytes accessed | tf_op | source)
XLA Modules:
  0.0 701.8 jit_solution(8970966009916328786)
XLA Ops:
  7.2 0.0 copy-start
  7.2 0.0 copy-start.4
  7.2 0.0 copy-start.6
  7.2 0.0 all-gather.3.cloned.1.call-start
  7.2 0.8 add_bitcast_fusion
  8.0 1.7 fusion.30
  9.7 0.0 all-gather.3.cloned.1.call-update
  9.8 0.0 all-gather.5.cloned.1.call-start
  9.8 2.7 convolution_convert_fusion.1
  12.5 0.0 all-gather.5.cloned.1.call-update
  12.5 0.0 reduce-scatter.2.cloned.1.call-start
  13.2 0.8 compare_select_fusion
  14.0 0.7 reduce
  14.7 0.6 iota_compare_fusion.1
  15.3 0.7 fusion.36
  16.7 0.0 copy-done.4
  16.7 0.9 copy.30
  17.6 0.0 copy-done.6
  17.7 0.0 copy-start.8
  17.7 0.0 copy-start.9
  17.7 65.4 %all-gather.3.cloned.1.call-done = bf16[768,1024]{1,0:T(8,128)(2,1)} async-done(((bf16[96,1024]{1,0:T(8,128)(2,1)}), bf16[768,1024]{1,0:T(8,128)(2,1)}) %all-gather.3.cloned.1.call-update) | async-done | bytes 1572880 | tf_op jit(solution)/shard_map/all_gather | solution.py:31
  83.1 9.4 %gather_fusion = bf16[1536,1024]{1,0:T(8,128)(2,1)} fusion(bf16[768,1024]{1,0:T(8,128)(2,1)} %all-gather.3.cloned.1.call-done, s32[2048]{0:T(1024)S(1)} %pad_clamp_fusion), kind=kCustom, calls=%fused_computation | custom fusion | bytes 6297600 | tf_op jit(solution)/shard_map/jit(_take)/gather | solution.py:46
  92.5 0.0 copy-done
  92.5 0.0 copy-done.8
  92.5 0.0 copy-done.9
  92.5 5.5 fusion.40
  98.0 52.9 %all-gather.5.cloned.1.call-done = bf16[12288,64]{0,1:T(8,128)(2,1)} async-done(((bf16[1536,64]{0,1:T(8,128)(2,1)}), bf16[12288,64]{0,1:T(8,128)(2,1)}) %all-gather.5.cloned.1.call-update) | async-done | bytes 1572880 | tf_op jit(solution)/shard_map/all_gather | solution.py:33
  150.9 4.1 copy.29
  155.0 74.9 %scatter_custom_fusion = f32[1536,64]{1,0:T(8,128)S(1)} fusion(s32[6144]{0:T(1024)S(1)} %bitcast.56, bf16[1,6144,64]{2,1,0:T(8,128)(2,1)S(1)} %copy.30, f32[]{:T(128)} %constant.38.clone.1, pred[6144]{0:T(1024)(128)(4,1)S(1)} %get-tuple-element.14, pred[6144]{0:T(1024)(128)(4,1)S(1)} %get-tuple-element.13, bf16[]{:T(256)} %constant.30.clone.1, ...), kind=kCustom, calls=%fused_computation.9 | custom fusion | flops 2359296 | bytes 5150208 | tf_op jit(solution)/shard_map/scatter-add | solution.py:39
  230.0 0.0 copy-start.7
  230.0 5.0 multiply_convert_fusion
  235.0 1.1 copy-done.2
  236.2 1.3 convolution_convert_fusion
  237.4 1.8 copy.31
  239.3 77.7 %scatter_custom_fusion.1 = f32[12288,64]{1,0:T(8,128)} fusion(s32[6144]{0:T(1024)S(1)} %bitcast.52, f32[]{:T(128)} %constant.38.clone.1, bf16[1,6144,64]{2,1,0:T(8,128)(2,1)S(1)} %copy.30, pred[6144]{0:T(1024)(128)(4,1)S(1)} %compare_and_fusion.1, pred[6144]{0:T(1024)(128)(4,1)S(1)} %get-tuple-element.13, bf16[]{:T(256)} %constant.30.clone.1, ...), kind=kCustom, calls=%fused_computation.11 | custom fusion | flops 2359296 | bytes 5150208 | tf_op jit(solution)/shard_map/scatter-add | solution.py:61
  317.0 4.2 convert_element_type.68
  321.1 0.0 reduce-scatter.2.cloned.1.call-update
  321.2 0.0 all-reduce.3.cloned.1.call-start
  321.2 2.6 fusion.32
  323.8 6.4 fusion.20
  330.2 94.1 %reduce-scatter.2.cloned.1.call-done = bf16[1536,64]{1,0:T(8,128)(2,1)} async-done(((bf16[12288,64]{1,0:T(8,128)(2,1)}), bf16[1536,64]{1,0:T(8,128)(2,1)}) %reduce-scatter.2.cloned.1.call-update) | async-done | bytes 196624 | tf_op jit(solution)/shard_map/reduce_scatter | solution.py:65
  424.3 2.1 fusion.25
  426.5 0.0 all-reduce.3.cloned.1.call-update
  426.5 3.6 fusion.10
  430.1 260.4 %all-reduce.3.cloned.1.call-done = (f32[512,1024]{1,0:T(8,128)}, f32[64,512]{1,0:T(8,128)}, f32[512,64]{0,1:T(8,128)}) async-done(((f32[512,1024]{1,0:T(8,128)}, f32[64,512]{1,0:T(8,128)}, f32[512,64]{0,1:T(8,128)}), (f32[512,1024]{1,0:T(8,128)}, f32[64,512]{1,0:T(8,128)}, f32[512,64]{0,1:T(8,128)})) %all-reduce.3.cloned.1.call-update) | async-done | bytes 2359312 | tf_op jit(solution)/shard_map/psum | solution.py:73
  690.5 1.7 constant_dynamic-slice_fusion
  692.2 1.6 copy.37
  693.7 1.6 copy.38
  (14 shorter events, 0.1 us)
Async XLA Ops:
  7.2 85.3 %copy-start = (bf16[512,1024]{1,0:T(8,128)(2,1)S(1)}, bf16[512,1024]{1,0:T(8,128)(2,1)}, u32[]{:S(2)}) copy-start(bf16[512,1024]{1,0:T(8,128)(2,1)} %param.23) | copy-start | bytes 3145732
  7.2 9.5 %copy-start.4 = (bf16[1,6144,64]{1,2,0:T(8,128)(2,1)S(1)}, bf16[1,6144,64]{1,2,0:T(8,128)(2,1)}, u32[]{:S(2)}) copy-start(bf16[1,6144,64]{1,2,0:T(8,128)(2,1)} %param.13) | copy-start | bytes 2359300
  7.2 10.4 %copy-start.6 = (s32[1,6144]{1,0:T(1,128)S(1)}, s32[1,6144]{1,0:T(1,128)}, u32[]{:S(2)}) copy-start(s32[1,6144]{1,0:T(1,128)} %param.17) | copy-start | bytes 73732
  7.2 75.9 %all-gather.3.cloned.1.call-start = ((), (), s32[]{:S(2)}) async-start(), calls=%async_computation.1 | async-start | bytes 1769472 | tf_op jit(solution)/shard_map/all_gather | solution.py:31
  9.8 141.2 %all-gather.5.cloned.1.call-start = ((), (), s32[]{:S(2)}) async-start(), calls=%async_computation.2 | async-start | bytes 1769472 | tf_op jit(solution)/shard_map/all_gather | solution.py:33
  12.5 411.8 %reduce-scatter.2.cloned.1.call-start = ((), (), s32[]{:S(2)}) async-start(), calls=%async_computation.3 | async-start | bytes 3538944 | tf_op jit(solution)/shard_map/reduce_scatter | solution.py:65
  17.7 74.8 %copy-start.8 = (pred[1536]{0:T(1024)(128)(4,1)S(1)}, pred[1536]{0:T(1024)(128)(4,1)}, u32[]{:S(2)}) copy-start(pred[1536]{0:T(1024)(128)(4,1)} %get-tuple-element.11) | copy-start | bytes 4612
  17.7 74.8 %copy-start.9 = (pred[1536]{0:T(1024)(128)(4,1)S(1)}, pred[1536]{0:T(1024)(128)(4,1)}, u32[]{:S(2)}) copy-start(pred[1536]{0:T(1024)(128)(4,1)} %get-tuple-element.12) | copy-start | bytes 4612
  230.0 6.2 copy-start.7
  235.0 1.1 copy-start.2
  321.1 2.7 copy-start.1
  321.2 369.3 %all-reduce.3.cloned.1.call-start = ((), (), s32[]{:S(2)}) async-start(), calls=%async_computation.4 | async-start | bytes 4718592 | tf_op jit(solution)/shard_map/psum | solution.py:73
  330.2 96.3 %copy-start.5 = (bf16[512,64]{0,1:T(8,128)(2,1)S(1)}, bf16[512,64]{0,1:T(8,128)(2,1)}, u32[]{:S(2)}) copy-start(bf16[512,64]{0,1:T(8,128)(2,1)} %param.21) | copy-start | bytes 196612
  424.3 2.2 copy-start.3
Sparse Core Ops, SparseCore 0:
  11.2 71.8 all-gather.2
  86.2 64.6 all-gather.4
  321.3 102.9 reduce-scatter.1
  430.4 259.9 all-reduce.2
where the time goes:
time: 703 us; the launch traced here: 702 us
  waiting for transfers between devices  473 us (67%)
  other arithmetic  162 us (23%)
  matrix products  29.2 us (4%)
  local copies, waits for them, and re-layouts  22.2 us (3%)
  between operations  15.2 us (2%)
    psum x1, waiting for transfers between devices, local(): lax.psum((part_atom, part_up, part_down), ('dp', 'graph'))  260 us
    reduce_scatter x1, waiting for transfers between devices, local(): lax.psum_scatter(partial_grad, 'graph', scatter_dimension=0, tiled=True)  94.1 us
    scatter-add x1, other arithmetic, local(): jax.ops.segment_sum(contrib, triplet_source[0], num_segments=edge_slots *...  77.7 us
    scatter-add x1, other arithmetic, local(): jax.ops.segment_sum(product, local_dest, num_segments=edge_slots)  74.9 us
    all_gather x1, waiting for transfers between devices, local(): atoms_all = lax.all_gather(scaled, 'graph', axis=0, tiled=True)  65.4 us
    all_gather x1, waiting for transfers between devices, local(): table = lax.all_gather(projected, 'graph', axis=0, tiled=True)  52.9 us
  transfers between devices with their start and end apart: 4, of which 4 were waited for; matrix products, arithmetic and copies ran while one was open for 5% of the time, Pallas kernels for 0%

commit v1 on v0

--- a/solution.py
+++ b/solution.py
@@ -30,7 +30,9 @@
     scaled = (weight[:, None] * atom_cotangent[0].astype(jnp.float32)).astype(jnp.bfloat16)
     atoms_all = lax.all_gather(scaled, "graph", axis=0, tiled=True)
     projected = jnp.dot(rows, w_down, preferred_element_type=jnp.float32).astype(jnp.bfloat16)
-    table = lax.all_gather(projected, "graph", axis=0, tiled=True)
+    table = jnp.concatenate(
+        lax.all_to_all(jnp.stack([projected] * lax.axis_size("graph")), "graph", 0, 0), axis=0
+    )
     feats = jnp.take(table, triplet_source[0], axis=0)
     local_dest = triplet_target[0] - here * edge_slots
     product = jnp.where(

time: 703 us -> 665 us (0.946)
  waiting for transfers between devices: 473 us -> 425 us
  starting transfers between devices: 0.16 us -> 11.2 us
    all_gather x1 -> x0, waiting for transfers between devices: 52.9 us -> none  [local(): table = lax.all_gather(projected, 'graph', axis=0, tiled=True)]
    all_to_all x0 -> x1, starting transfers between devices: none -> 11.1 us  [local(): lax.all_to_all(jnp.stack([projected] * lax.axis_size('graph')), 'graph',...]
  transfers between devices with their start and end apart: 4 -> 4, of which waited for: 4 -> 3; matrix products, arithmetic and copies ran while one was open for 5% -> 5% of each run, Pallas kernels for 0% -> 0%
where the time goes in v1:
time: 665 us; the launch traced here: 664 us
  waiting for transfers between devices  425 us (64%)
  other arithmetic  160 us (24%)
  matrix products  28.5 us (4%)
  local copies, waits for them, and re-layouts  23.5 us (4%)
  between operations  15.2 us (2%)
  starting transfers between devices  11.2 us (2%)
    psum x1, waiting for transfers between devices, local(): lax.psum((part_atom, part_up, part_down), ('dp', 'graph'))  261 us
    reduce_scatter x1, waiting for transfers between devices, local(): lax.psum_scatter(partial_grad, 'graph', scatter_dimension=0, tiled=True)  96.8 us
    scatter-add x1, other arithmetic, local(): jax.ops.segment_sum(contrib, triplet_source[0], num_segments=edge_slots *...  77.6 us
    scatter-add x1, other arithmetic, local(): jax.ops.segment_sum(product, local_dest, num_segments=edge_slots)  75 us
    all_gather x1, waiting for transfers between devices, local(): atoms_all = lax.all_gather(scaled, 'graph', axis=0, tiled=True)  67.8 us
  transfers between devices with their start and end apart: 4, of which 3 were waited for; matrix products, arithmetic and copies ran while one was open for 5% of the time, Pallas kernels for 0%

profile of v1, /device:TPU:8, one launch (start us, length us, event | category | flops | bytes accessed | tf_op | source)
XLA Modules:
  0.0 663.7 jit_solution(7014523695578359783)
XLA Ops:
  7.2 0.0 copy-start
  7.2 0.0 all-gather.2.cloned.1.call-start
  7.2 0.7 add_bitcast_fusion
  8.0 1.7 fusion.30
  9.7 0.0 all-gather.2.cloned.1.call-update
  9.7 0.0 copy-start.9
  9.7 0.0 copy-start.8
  9.7 0.0 copy-start.4
  9.7 2.1 convolution_convert_fusion.1
  11.8 1.3 stack.2
  13.1 11.1 %all-to-all-start = ((bf16[8,1536,64]{1,2,0:T(8,128)(2,1)}), bf16[8,1536,64]{1,2,0:T(8,128)(2,1)}, u32[]{:S(2)}, u32[]{:S(2)}) async-start(bf16[8,1536,64]{1,2,0:T(8,128)(2,1)} %stack.2), calls=%async_computation | async-start | bytes 3145728 | tf_op jit(solution)/shard_map/all_to_all | solution.py:34
  24.1 0.0 reduce-scatter.2.cloned.1.call-start
  24.2 0.0 copy-done.9
  24.9 0.0 copy-done.8
  24.9 0.6 iota_compare_fusion.1
  26.2 0.0 copy-done.4
  26.2 0.9 copy.33
  27.1 0.0 copy-done.6
  27.2 0.0 copy-start.10
  27.2 0.0 copy-start.11
  27.2 67.8 %all-gather.2.cloned.1.call-done = bf16[768,1024]{1,0:T(8,128)(2,1)} async-done(((bf16[96,1024]{1,0:T(8,128)(2,1)}), bf16[768,1024]{1,0:T(8,128)(2,1)}) %all-gather.2.cloned.1.call-update) | async-done | bytes 1572880 | tf_op jit(solution)/shard_map/all_gather | solution.py:31
  95.1 9.4 %gather_fusion = bf16[1536,1024]{1,0:T(8,128)(2,1)} fusion(bf16[768,1024]{1,0:T(8,128)(2,1)} %all-gather.2.cloned.1.call-done, s32[2048]{0:T(1024)S(1)} %pad_clamp_fusion), kind=kCustom, calls=%fused_computation | custom fusion | bytes 6297600 | tf_op jit(solution)/shard_map/jit(_take)/gather | solution.py:48
  104.4 0.0 copy-done
  104.5 0.0 copy-done.10
  104.5 5.5 fusion.40
  109.9 0.0 all-to-all-done
  109.9 4.1 copy.32
  114.1 75.0 %scatter_custom_fusion = f32[1536,64]{1,0:T(8,128)S(1)} fusion(s32[6144]{0:T(1024)S(1)} %bitcast.58, bf16[1,6144,64]{2,1,0:T(8,128)(2,1)S(1)} %copy.33, f32[]{:T(128)} %constant.38.clone.1, pred[6144]{0:T(1024)(128)(4,1)S(1)} %get-tuple-element.14, pred[6144]{0:T(1024)(128)(4,1)S(1)} %get-tuple-element.13, bf16[]{:T(256)} %constant.30.clone.1, ...), kind=kCustom, calls=%fused_computation.9 | custom fusion | flops 2359296 | bytes 5150208 | tf_op jit(solution)/shard_map/scatter-add | solution.py:41
  189.0 0.0 copy-start.7
  189.0 5.0 multiply_convert_fusion
  194.1 1.1 copy-done.2
  195.2 0.0 copy-done.7
  195.2 1.3 convolution_convert_fusion
  196.5 1.9 copy.34
  198.3 77.6 %scatter_custom_fusion.1 = f32[12288,64]{1,0:T(8,128)} fusion(s32[6144]{0:T(1024)S(1)} %bitcast.54, f32[]{:T(128)} %constant.38.clone.1, bf16[1,6144,64]{2,1,0:T(8,128)(2,1)S(1)} %copy.33, pred[6144]{0:T(1024)(128)(4,1)S(1)} %compare_and_fusion.1, pred[6144]{0:T(1024)(128)(4,1)S(1)} %get-tuple-element.13, bf16[]{:T(256)} %constant.30.clone.1, ...), kind=kCustom, calls=%fused_computation.11 | custom fusion | flops 2359296 | bytes 5150208 | tf_op jit(solution)/shard_map/scatter-add | solution.py:63
  276.0 4.2 convert_element_type.68
  280.1 0.0 reduce-scatter.2.cloned.1.call-update
  280.1 0.0 all-reduce.3.cloned.1.call-start
  280.2 2.6 fusion.32
  282.8 6.4 fusion.20
  289.2 96.8 %reduce-scatter.2.cloned.1.call-done = bf16[1536,64]{1,0:T(8,128)(2,1)} async-done(((bf16[12288,64]{1,0:T(8,128)(2,1)}), bf16[1536,64]{1,0:T(8,128)(2,1)}) %reduce-scatter.2.cloned.1.call-update) | async-done | bytes 196624 | tf_op jit(solution)/shard_map/reduce_scatter | solution.py:67
  386.0 2.1 fusion.25
  388.1 0.0 all-reduce.3.cloned.1.call-update
  388.2 3.6 fusion.10
  391.8 260.6 %all-reduce.3.cloned.1.call-done = (f32[512,1024]{1,0:T(8,128)}, f32[64,512]{1,0:T(8,128)}, f32[512,64]{0,1:T(8,128)}) async-done(((f32[512,1024]{1,0:T(8,128)}, f32[64,512]{1,0:T(8,128)}, f32[512,64]{0,1:T(8,128)}), (f32[512,1024]{1,0:T(8,128)}, f32[64,512]{1,0:T(8,128)}, f32[512,64]{0,1:T(8,128)})) %all-reduce.3.cloned.1.call-update) | async-done | bytes 2359312 | tf_op jit(solution)/shard_map/psum | solution.py:75
  652.4 1.7 constant_dynamic-slice_fusion
  654.1 1.6 copy.40
  655.6 1.6 copy.41
  (18 shorter events, 0.2 us)
Async XLA Ops:
  7.2 97.3 %copy-start = (bf16[512,1024]{1,0:T(8,128)(2,1)S(1)}, bf16[512,1024]{1,0:T(8,128)(2,1)}, u32[]{:S(2)}) copy-start(bf16[512,1024]{1,0:T(8,128)(2,1)} %param.23) | copy-start | bytes 3145732
  7.2 87.9 %all-gather.2.cloned.1.call-start = ((), (), s32[]{:S(2)}) async-start(), calls=%async_computation.2 | async-start | bytes 1769472 | tf_op jit(solution)/shard_map/all_gather | solution.py:31
  9.7 14.5 %copy-start.9 = (s32[1,6144]{1,0:T(1,128)S(1)}, s32[1,6144]{1,0:T(1,128)}, u32[]{:S(2)}) copy-start(s32[1,6144]{1,0:T(1,128)} %param.18) | copy-start | bytes 73732
  9.7 15.2 %copy-start.8 = (s32[1,1536]{1,0:T(1,128)S(1)}, s32[1,1536]{1,0:T(1,128)}, u32[]{:S(2)}) copy-start(s32[1,1536]{1,0:T(1,128)} %param.16) | copy-start | bytes 18436
  9.7 16.5 %copy-start.4 = (bf16[1,6144,64]{1,2,0:T(8,128)(2,1)S(1)}, bf16[1,6144,64]{1,2,0:T(8,128)(2,1)}, u32[]{:S(2)}) copy-start(bf16[1,6144,64]{1,2,0:T(8,128)(2,1)} %param.13) | copy-start | bytes 2359300
  13.1 14.0 %copy-start.6 = (s32[1,6144]{1,0:T(1,128)S(1)}, s32[1,6144]{1,0:T(1,128)}, u32[]{:S(2)}) copy-start(s32[1,6144]{1,0:T(1,128)} %param.17) | copy-start | bytes 73732
  13.1 96.8 %all-to-all-start = ((bf16[8,1536,64]{1,2,0:T(8,128)(2,1)}), bf16[8,1536,64]{1,2,0:T(8,128)(2,1)}, u32[]{:S(2)}, u32[]{:S(2)}) async-start(bf16[8,1536,64]{1,2,0:T(8,128)(2,1)} %stack.2), calls=%async_computation | async-start | bytes 3145728 | tf_op jit(solution)/shard_map/all_to_all | solution.py:34
  24.1 361.9 %reduce-scatter.2.cloned.1.call-start = ((), (), s32[]{:S(2)}) async-start(), calls=%async_computation.3 | async-start | bytes 3538944 | tf_op jit(solution)/shard_map/reduce_scatter | solution.py:67
  27.2 77.2 %copy-start.10 = (pred[1536]{0:T(1024)(128)(4,1)S(1)}, pred[1536]{0:T(1024)(128)(4,1)}, u32[]{:S(2)}) copy-start(pred[1536]{0:T(1024)(128)(4,1)} %get-tuple-element.11) | copy-start | bytes 4612
  27.2 77.2 %copy-start.11 = (pred[1536]{0:T(1024)(128)(4,1)S(1)}, pred[1536]{0:T(1024)(128)(4,1)}, u32[]{:S(2)}) copy-start(pred[1536]{0:T(1024)(128)(4,1)} %get-tuple-element.12) | copy-start | bytes 4612
  189.0 6.2 copy-start.7
  194.1 1.1 copy-start.2
  280.1 2.7 copy-start.1
  280.1 372.2 %all-reduce.3.cloned.1.call-start = ((), (), s32[]{:S(2)}) async-start(), calls=%async_computation.4 | async-start | bytes 4718592 | tf_op jit(solution)/shard_map/psum | solution.py:75
  289.2 99.0 %copy-start.5 = (bf16[512,64]{0,1:T(8,128)(2,1)S(1)}, bf16[512,64]{0,1:T(8,128)(2,1)}, u32[]{:S(2)}) copy-start(bf16[512,64]{0,1:T(8,128)(2,1)} %param.21) | copy-start | bytes 196612
  386.0 2.2 copy-start.3
Sparse Core Ops, SparseCore 0:
  11.2 83.8 all-gather.1
  280.3 105.6 reduce-scatter.1
  392.3 260.0 all-reduce.2
